TPU v7x, 256 devices: a whole 4x4x8 slice. The times are simulated.
256 devices in a mesh: space: 32 (over z, x), mode: 8 (over y, core).
Axes of the slice: x: 4, y: 4, z: 8, core: 2. Of those that a mesh axis runs over, the one named last changes fastest.
Arguments:
- vectors: float32 [55296, 256], P('space', 'mode'), may hold values from -6 to 6
- force_blocks: float32 [288, 27, 192, 192], P('space', None, 'mode'), as said below
- inverse_blocks: float32 [288, 192, 192], P('space'), as said below
- neighbours: int32 [288, 27], P('space'), may hold values from 0 to 287, as said below
Outputs:
- w_block: float32 [55296, 256], P('space', 'mode')
- hw_block: float32 [55296, 256], P('space', 'mode')
- gram_a: float32 [512, 2, 256], P(None, None, 'mode')
- gram_b: float32 [512, 2, 256], P(None, None, 'mode')
Inputs may be any that keep to these rules, and one draw needn't show every extreme that they name: `neighbours`: block rows are atom cells on a periodic grid of 32 layers of 3 x 3 cells; the rows of layer z are z * 9 to z * 9 + 8 in some order. Entry k = 9 (dz + 1) + 3 (dy + 1) + (dx + 1) of row i is the block row of the cell at offset (dz, dy, dx) from row i's cell, so entry 13 is i itself. H is symmetric: force_blocks[neighbours[i, k], 26 - k] is the transpose of force_blocks[i, k]. `inverse_blocks`: every block is symmetric.
All inputs are finite; a program needn't handle non-finite values.
Results may differ from a plain program's by a relative error of at most 0.00013.
Values sent between devices are 32-bit elements; how exact they have to be, the bound alone decides.
No kernel may reach another device: no remote copies, remote signals or barrier semaphores. Data moves between devices by JAX's collectives and lax.ppermute only.
A program may use at most 128 MiB of HBM per device.

v0:
```python
import jax
import jax.numpy as jnp
from jax import lax
from jax.sharding import PartitionSpec as P

CELLS = 9
HIGHEST = lax.Precision.HIGHEST


def space_sum(value):
    count = lax.axis_size("space")
    step = 1
    while step < count:
        pairs = [(i, i ^ step) for i in range(count)]
        value = value + lax.ppermute(value, "space", pairs)
        step *= 2
    return value


def halo(block, width):
    count = lax.axis_size("space")
    forward = [(i, (i + 1) % count) for i in range(count)]
    backward = [((i + 1) % count, i) for i in range(count)]
    low = lax.ppermute(block[block.shape[0] - width :], "space", forward)
    high = lax.ppermute(block[:width], "space", backward)
    return (low, high)


def dense_rows(force_blocks, local_ids, ext_blocks):
    block_rows, neigh = local_ids.shape
    columns = jnp.arange(ext_blocks, dtype=jnp.int32)
    onehot = local_ids[:, :, None] == columns[None, None, :]
    offsets = jnp.arange(neigh, dtype=jnp.int32)
    which = jnp.sum(jnp.where(onehot, offsets[None, :, None], 0), axis=1)
    valid = jnp.any(onehot, axis=1)
    flat = (jnp.arange(block_rows, dtype=jnp.int32)[:, None] * neigh + which).reshape(-1)
    rows, cols = (force_blocks.shape[2], force_blocks.shape[3])
    table = force_blocks.reshape(block_rows * neigh, rows * cols)
    picked = jnp.take(table, flat, axis=0).reshape(block_rows, ext_blocks, rows, cols)
    return jnp.where(valid[:, :, None, None], picked, 0.0)


def apply_dense(dense, low, own, high):
    width = low.shape[0]
    own_count = own.shape[0]
    parts = (
        (dense[:, width : width + own_count], own),
        (dense[:, :width], low),
        (dense[:, width + own_count :], high),
    )
    total = None
    for coeffs, field in parts:
        product = jnp.einsum(
            "ijrc,jcm->irm", coeffs, field, precision=HIGHEST, preferred_element_type=jnp.float32
        )
        total = product if total is None else total + product
    regrouped = lax.all_to_all(total, "mode", split_axis=2, concat_axis=1, tiled=True)
    return regrouped.reshape(-1, regrouped.shape[2])


def local(vectors, force_blocks, inverse_blocks, neighbours):
    row_count, col_count = vectors.shape
    block_size = inverse_blocks.shape[1]
    block_rows = row_count // block_size
    slab_count = lax.axis_size("space")
    total_rows = row_count * slab_count
    own_layers = block_rows // CELLS
    layer_total = own_layers * slab_count
    slab_index = lax.axis_index("space")
    mode_index = lax.axis_index("mode")
    layer_of = neighbours // CELLS
    relative = (layer_of - slab_index * own_layers + 1) % layer_total
    local_ids = relative * CELLS + neighbours % CELLS
    ext_blocks = block_rows + 2 * CELLS
    dense = dense_rows(force_blocks, local_ids, ext_blocks)
    stacked_x = vectors.reshape(block_rows, block_size, col_count)
    full_x = lax.all_gather(stacked_x, "mode", axis=2, tiled=True)
    low_x, high_x = halo(full_x, CELLS)
    image_x = apply_dense(dense, low_x, full_x, high_x)
    mode_count = full_x.shape[2]
    flat_x = full_x.reshape(row_count, mode_count)
    rayleigh = (
        space_sum(
            jnp.einsum(
                "ra,rj->aj", flat_x, image_x, precision=HIGHEST, preferred_element_type=jnp.float32
            )
        )
        / total_rows
    )
    residual = image_x - jnp.dot(
        flat_x, rayleigh, precision=HIGHEST, preferred_element_type=jnp.float32
    )
    search_raw = jnp.einsum(
        "brc,bcm->brm",
        inverse_blocks,
        residual.reshape(block_rows, block_size, col_count),
        precision=HIGHEST,
        preferred_element_type=jnp.float32,
    )
    full_s = lax.all_gather(search_raw, "mode", axis=2, tiled=True)
    low_s, high_s = halo(full_s, CELLS)
    image_s = apply_dense(dense, low_s, full_s, high_s)
    flat_s = full_s.reshape(row_count, mode_count)
    own_s = search_raw.reshape(row_count, col_count)
    squares = jnp.sum(flat_s * flat_s, axis=0)
    basis = jnp.concatenate([flat_x, flat_s], axis=1)
    columns = jnp.stack([vectors, own_s, image_x, image_s], axis=1)
    gram_part = jnp.einsum(
        "ra,rgj->agj", basis, columns, precision=HIGHEST, preferred_element_type=jnp.float32
    )
    packed = jnp.concatenate([gram_part.reshape(-1), squares])
    summed = space_sum(packed)
    gram_sum = summed[: gram_part.size].reshape(gram_part.shape)
    scales_all = lax.rsqrt(summed[gram_part.size :] / total_rows + 1e-06)
    scales_own = lax.dynamic_slice_in_dim(scales_all, mode_index * col_count, col_count)
    w_block = own_s * scales_own
    hw_block = image_s * scales_own
    row_scale = jnp.concatenate([jnp.ones((mode_count,), jnp.float32), scales_all])
    ones_own = jnp.ones((col_count,), jnp.float32)
    col_scale = jnp.stack([ones_own, scales_own, ones_own, scales_own])
    gram = gram_sum * row_scale[:, None, None] * col_scale[None] / total_rows
    gram_b = gram[:, 0:2]
    gram_a = gram[:, 2:4]
    return (w_block, hw_block, gram_a, gram_b)


def solution(mesh):
    in_specs = (
        P("space", "mode"),
        P("space", None, "mode", None),
        P("space", None, None),
        P("space", None),
    )
    out_specs = (
        P("space", "mode"),
        P("space", "mode"),
        P(None, None, "mode"),
        P(None, None, "mode"),
    )
    return jax.shard_map(local, mesh=mesh, in_specs=in_specs, out_specs=out_specs, check_vma=False)
```

profile of v0, /device:TPU:2, one launch (start us, length us, event | category | flops | bytes accessed | tf_op | source)
XLA Modules:
  0.0 340.8 jit_solution(18224668722310381705)
XLA Ops:
  7.2 1.2 reshape.103
  8.4 0.9 copy.49
  9.4 31.6 %all-gather.3.cloned.1.call-done = f32[9,192,256]{1,2,0:T(8,128)} async-done(((f32[9,192,32]{1,2,0:T(8,128)}), f32[9,192,256]{1,2,0:T(8,128)}) %all-gather.3.cloned.1.call-update) | async-done | bytes 1769488 | tf_op jit(solution)/shard_map/all_gather | solution.py:77
  41.0 2.0 copy.50
  43.0 1.5 collective-permute-start
  46.7 6.7 %reshape.102 = f32[243,4608]{1,0:T(8,128)} reshape(f32[9,27,24,192]{3,2,1,0:T(8,128)} %param.5) | data formatting | bytes 8957952 | tf_op jit(solution)/shard_map/reshape | solution.py:38
  53.5 8.4 %gather_fusion = f32[243,4608]{1,0:T(8,128)} fusion(f32[243,4608]{1,0:T(8,128)} %reshape.102, s32[1024]{0:T(1024)S(1)} %pad_clamp_fusion), kind=kCustom, calls=%fused_computation | custom fusion | bytes 8958924 | tf_op jit(solution)/shard_map/jit(_take)/gather | solution.py:39
  61.9 6.9 %gather.7 = f32[9,27,24,192]{3,2,1,0:T(8,128)} reshape(f32[243,4608]{1,0:T(8,128)} %gather_fusion) | data formatting | bytes 8957952 | tf_op jit(solution)/shard_map/jit(_take)/gather | solution.py:39
  68.9 4.6 %fusion.19 = f32[9,24,256]{2,1,0:T(8,128)S(1)} fusion(f32[9,192,256]{1,2,0:T(8,128)} %all-gather.3.cloned.1.call-done, f32[9,27,24,192]{3,2,1,0:T(8,128)} %gather.7, pred[9,27]{1,0:T(8,128)(4,1)S(1)} %get-tuple-element.16, pred[9,27]{1,0:T(8,128)(4,1)S(1)} %fusion.47), kind=kOutput, calls=%fused_computation.25 | convolution fusion | flops 1148857344 | bytes 6470118 | tf_op jit(solution)/shard_map/ijrc,jcm->irm/dot_general | solution.py:53
  73.5 10.4 %collective-permute-done = f32[9,192,256]{2,1,0:T(8,128)} collective-permute-done((f32[9,192,256]{2,1,0:T(8,128)S(1)}, f32[9,192,256]{2,1,0:T(8,128)}, u32[]{:S(2)}, u32[]{:S(2)}) %collective-permute-start) | collective-permute-done | bytes 1769504 | tf_op jit(solution)/shard_map/ppermute | solution.py:24
  83.9 3.5 %fusion.37 = f32[9,24,256]{2,1,0:T(8,128)S(1)} fusion(f32[9,24,256]{2,1,0:T(8,128)S(1)} %fusion.19, f32[9,192,256]{2,1,0:T(8,128)} %collective-permute-done, f32[9,27,24,192]{3,2,1,0:T(8,128)S(1)} %copy-done.1, pred[9,27]{1,0:T(8,128)(4,1)S(1)} %get-tuple-element.16, pred[9,27]{1,0:T(8,128)(4,1)S(1)} %fusion.47), kind=kOutput, calls=%fused_computation.31 | convolution fusion | flops 1148912640 | bytes 6691302 | tf_op jit(solution)/shard_map/ijrc,jcm->irm/dot_general | solution.py:53
  87.4 4.2 %fusion.34 = f32[9,24,256]{2,1,0:T(8,128)} fusion(f32[9,24,256]{2,1,0:T(8,128)S(1)} %fusion.37, f32[9,192,256]{2,1,0:T(8,128)} %collective-permute-done.1, f32[9,27,24,192]{3,2,1,0:T(8,128)S(1)} %copy-done.1, pred[9,27]{1,0:T(8,128)(4,1)S(1)} %get-tuple-element.16, pred[9,27]{1,0:T(8,128)(4,1)S(1)} %fusion.47), kind=kOutput, calls=%fused_computation.30 | convolution fusion | flops 1148912640 | bytes 6691302 | tf_op jit(solution)/shard_map/ijrc,jcm->irm/dot_general | solution.py:53
  91.6 3.4 copy.52
  95.0 3.1 reshape.133
  98.1 11.1 %all_to_all.30 = f32[8,1,6912]{2,1,0:T(1,128)} all-to-all(f32[8,1,6912]{2,1,0:T(1,128)} %reshape.133), channel_id=1, replica_groups=mesh['space'=32,'mode'=8] {'mode'}, dimensions={0} | all-to-all | bytes 442368 | tf_op jit(solution)/shard_map/all_to_all | solution.py:57
  109.7 2.8 reduce.1
  112.5 2.8 reshape.134
  115.3 3.3 copy.77
  118.6 2.3 reshape.104
  120.9 1.9 convolution_bitcast_fusion.3
  122.8 4.3 %collective-permute-start.2 = (f32[256,32]{0,1:T(8,128)S(1)}, f32[256,32]{0,1:T(8,128)S(1)}, u32[]{:S(2)}, u32[]{:S(2)}) collective-permute-start(f32[256,32]{0,1:T(8,128)S(1)} %convolution_bitcast_fusion.3), channel_id=1, source_target_pairs={{0,8},{8,0},{16,24},{24,16},{32,40},{40,32},{48,56},{56,48},{64,72... | collective-permute-start | bytes 98312 | tf_op jit(solution)/shard_map/ppermute | solution.py:15
  127.2 1.9 collective-permute-done.2
  129.1 5.4 %collective-permute-done.3 = f32[256,32]{0,1:T(8,128)S(1)} collective-permute-done((f32[256,32]{0,1:T(8,128)S(1)}, f32[256,32]{0,1:T(8,128)S(1)}, u32[]{:S(2)}, u32[]{:S(2)}) %collective-permute-start.3) | collective-permute-done | bytes 32800 | tf_op jit(solution)/shard_map/ppermute | solution.py:15
  134.7 3.9 %collective-permute-done.4 = f32[256,32]{0,1:T(8,128)S(1)} collective-permute-done((f32[256,32]{0,1:T(8,128)S(1)}, f32[256,32]{0,1:T(8,128)S(1)}, u32[]{:S(2)}, u32[]{:S(2)}) %collective-permute-start.4) | collective-permute-done | bytes 32800 | tf_op jit(solution)/shard_map/ppermute | solution.py:15
  138.6 0.9 collective-permute-start.5
  139.5 3.9 %collective-permute-done.5 = f32[256,32]{0,1:T(8,128)S(1)} collective-permute-done((f32[256,32]{0,1:T(8,128)S(1)}, f32[256,32]{0,1:T(8,128)S(1)}, u32[]{:S(2)}, u32[]{:S(2)}) %collective-permute-start.5) | collective-permute-done | bytes 32800 | tf_op jit(solution)/shard_map/ppermute | solution.py:15
  143.4 5.4 %collective-permute-start.6 = (f32[256,32]{0,1:T(8,128)S(1)}, f32[256,32]{0,1:T(8,128)S(1)}, u32[]{:S(2)}, u32[]{:S(2)}) collective-permute-start(f32[256,32]{0,1:T(8,128)S(1)} %add.131), channel_id=1, source_target_pairs={{0,128},{8,136},{16,144},{24,152},{32,160},{40,168},{48,176},{56,1... | collective-permute-start | bytes 98312 | tf_op jit(solution)/shard_map/ppermute | solution.py:15
  148.8 2.4 collective-permute-done.6
  151.2 2.3 fusion.11
  153.6 1.1 reshape.106
  154.6 2.4 convolution_bitcast_fusion.2
  157.1 26.9 %all-gather.5.cloned.1.call-done = f32[9,192,256]{1,2,0:T(8,128)} async-done(((f32[9,192,32]{1,2,0:T(8,128)}), f32[9,192,256]{1,2,0:T(8,128)}) %all-gather.5.cloned.1.call-update) | async-done | bytes 1769488 | tf_op jit(solution)/shard_map/all_gather | solution.py:100
  184.0 3.0 copy.57
  187.0 1.5 collective-permute-start.7
  189.2 1.0 stack_reshape.10
  190.2 1.0 copy.56
  191.2 2.0 stack_reshape.9
  193.2 4.6 %fusion.16 = f32[9,24,256]{2,1,0:T(8,128)S(1)} fusion(f32[9,192,256]{1,2,0:T(8,128)} %all-gather.5.cloned.1.call-done, f32[9,27,24,192]{3,2,1,0:T(8,128)} %gather.7, pred[9,27]{1,0:T(8,128)(4,1)S(1)} %get-tuple-element.16, pred[9,27]{1,0:T(8,128)(4,1)S(1)} %fusion.47), kind=kOutput, calls=%fused_computation.24 | convolution fusion | flops 1148857344 | bytes 6470118 | tf_op jit(solution)/shard_map/ijrc,jcm->irm/dot_general | solution.py:53
  197.9 30.2 %collective-permute-done.7 = f32[9,192,256]{2,1,0:T(8,128)} collective-permute-done((f32[9,192,256]{2,1,0:T(8,128)}, f32[9,192,256]{2,1,0:T(8,128)}, u32[]{:S(2)}, u32[]{:S(2)}) %collective-permute-start.7) | collective-permute-done | bytes 1769504 | tf_op jit(solution)/shard_map/ppermute | solution.py:24
  228.0 4.0 %fusion.43 = f32[9,24,256]{2,1,0:T(8,128)S(1)} fusion(f32[9,24,256]{2,1,0:T(8,128)S(1)} %fusion.16, f32[9,192,256]{2,1,0:T(8,128)} %collective-permute-done.7, f32[9,27,24,192]{3,2,1,0:T(8,128)} %gather.7, pred[9,27]{1,0:T(8,128)(4,1)S(1)} %get-tuple-element.16, pred[9,27]{1,0:T(8,128)(4,1)S(1)} %fusion.47), kind=kOutput, calls=%fused_computation.33 | convolution fusion | flops 1148912640 | bytes 6691302 | tf_op jit(solution)/shard_map/ijrc,jcm->irm/dot_general | solution.py:53
  232.1 4.1 %fusion.40 = f32[9,24,256]{2,1,0:T(8,128)} fusion(f32[9,24,256]{2,1,0:T(8,128)S(1)} %fusion.43, f32[9,192,256]{2,1,0:T(8,128)} %collective-permute-done.8, f32[9,27,24,192]{3,2,1,0:T(8,128)S(1)} %bitcast.126, pred[9,27]{1,0:T(8,128)(4,1)S(1)} %get-tuple-element.16, pred[9,27]{1,0:T(8,128)(4,1)S(1)} %fusion.47), kind=kOutput, calls=%fused_computation.32 | convolution fusion | flops 1148912640 | bytes 6691302 | tf_op jit(solution)/shard_map/ijrc,jcm->irm/dot_general | solution.py:53
  236.2 3.4 copy.61
  239.6 3.1 reshape.135
  242.7 3.8 %all-to-all-start.1 = ((f32[8,1,6912]{2,1,0:T(1,128)}), f32[8,1,6912]{2,1,0:T(1,128)S(1)}, u32[]{:S(2)}, u32[]{:S(2)}) async-start(f32[8,1,6912]{2,1,0:T(1,128)} %reshape.135), calls=%async_computation.1 | async-start | bytes 442368 | tf_op jit(solution)/shard_map/all_to_all | solution.py:57
  246.5 1.9 multiply_reduce_fusion
  248.5 5.1 %all-to-all-done.1 = f32[8,1,6912]{2,1,0:T(1,128)S(1)} async-done(((f32[8,1,6912]{2,1,0:T(1,128)}), f32[8,1,6912]{2,1,0:T(1,128)S(1)}, u32[]{:S(2)}, u32[]{:S(2)}) %all-to-all-start.1) | async-done | bytes 221216 | tf_op jit(solution)/shard_map/all_to_all | solution.py:57
  253.6 1.2 reduce.2
  254.7 1.9 reshape.136
  256.6 3.3 copy.76
  259.9 2.4 stack_reshape.11
  262.4 1.3 pad_maximum_fusion
  263.7 7.3 %convolution_bitcast_fusion = f32[65536]{0:T(1024)S(1)} fusion(f32[1728,128]{0,1:T(8,128)S(1)} %bitcast.139, f32[1728,256]{1,0:T(8,128)} %bitcast.138, f32[1728,256]{1,0:T(8,128)S(1)} %bitcast.129), kind=kOutput, calls=%fused_computation.1 | convolution fusion | flops 1359839232 | bytes 4685824
  271.1 4.3 %collective-permute-start.9 = (f32[65792]{0:T(1024)S(1)}, f32[65792]{0:T(1024)S(1)}, u32[]{:S(2)}, u32[]{:S(2)}) collective-permute-start(f32[65792]{0:T(1024)S(1)} %pad_maximum_fusion.1), channel_id=1, source_target_pairs={{0,8},{8,0},{16,24},{24,16},{32,40},{40,32},{48,56},{56,48},{64,72... | collective-permute-start | bytes 789512 | tf_op jit(solution)/shard_map/ppermute | solution.py:15
  275.5 6.1 %collective-permute-done.9 = f32[65792]{0:T(1024)S(1)} collective-permute-done((f32[65792]{0:T(1024)S(1)}, f32[65792]{0:T(1024)S(1)}, u32[]{:S(2)}, u32[]{:S(2)}) %collective-permute-start.9) | collective-permute-done | bytes 263200 | tf_op jit(solution)/shard_map/ppermute | solution.py:15
  281.7 8.7 %collective-permute-done.10 = f32[65792]{0:T(1024)S(1)} collective-permute-done((f32[65792]{0:T(1024)S(1)}, f32[65792]{0:T(1024)S(1)}, u32[]{:S(2)}, u32[]{:S(2)}) %collective-permute-start.10) | collective-permute-done | bytes 263200 | tf_op jit(solution)/shard_map/ppermute | solution.py:15
  290.6 6.4 %collective-permute-done.11 = f32[65792]{0:T(1024)S(1)} collective-permute-done((f32[65792]{0:T(1024)S(1)}, f32[65792]{0:T(1024)S(1)}, u32[]{:S(2)}, u32[]{:S(2)}) %collective-permute-start.11) | collective-permute-done | bytes 263200 | tf_op jit(solution)/shard_map/ppermute | solution.py:15
  297.0 1.0 collective-permute-start.12
  298.1 10.9 %collective-permute-done.12 = f32[65792]{0:T(1024)S(1)} collective-permute-done((f32[65792]{0:T(1024)S(1)}, f32[65792]{0:T(1024)S(1)}, u32[]{:S(2)}, u32[]{:S(2)}) %collective-permute-start.12) | collective-permute-done | bytes 263200 | tf_op jit(solution)/shard_map/ppermute | solution.py:15
  309.7 5.6 %collective-permute-start.13 = (f32[65792]{0:T(1024)}, f32[65792]{0:T(1024)}, u32[]{:S(2)}, u32[]{:S(2)}) collective-permute-start(f32[65792]{0:T(1024)} %add.138), channel_id=1, source_target_pairs={{0,128},{8,136},{16,144},{24,152},{32,160},{40,168},{48,176},{56,1... | collective-permute-start | bytes 789512 | tf_op jit(solution)/shard_map/ppermute | solution.py:15
  316.5 10.9 %collective-permute-done.13 = f32[65792]{0:T(1024)} collective-permute-done((f32[65792]{0:T(1024)}, f32[65792]{0:T(1024)}, u32[]{:S(2)}, u32[]{:S(2)}) %collective-permute-start.13) | collective-permute-done | bytes 263200 | tf_op jit(solution)/shard_map/ppermute | solution.py:15
  327.4 1.1 add.139
  329.1 1.5 multiply_multiply_fusion
  331.1 0.8 copy.64
  332.8 0.9 broadcast_multiply_fusion
  (69 shorter events, 8.0 us)
Async XLA Ops:
  7.2 147.5 %copy-start = (f32[9,192,192]{2,1,0:T(8,128)S(1)}, f32[9,192,192]{2,1,0:T(8,128)}, u32[]{:S(2)}) copy-start(f32[9,192,192]{2,1,0:T(8,128)} %param.6) | copy-start | bytes 3981316
  7.2 33.8 %all-gather.3.cloned.1.call-start = ((), (), s32[]{:S(2)}) async-start(), calls=%async_computation.2 | async-start | bytes 2654208 | tf_op jit(solution)/shard_map/all_gather | solution.py:77
  9.3 35.8 %copy-start.10 = (s32[9,27]{1,0:T(8,128)S(1)}, s32[9,27]{1,0:T(8,128)}, u32[]{:S(2)}) copy-start(s32[9,27]{1,0:T(8,128)} %param.7) | copy-start | bytes 2920
  9.3 174.6 %all-gather.5.cloned.1.call-start = ((), (), s32[]{:S(2)}) async-start(), calls=%async_computation.3 | async-start | bytes 2654208 | tf_op jit(solution)/shard_map/all_gather | solution.py:100
  43.0 108.2 %copy-start.2 = (f32[9,192,256]{2,1,0:T(8,128)}, f32[9,192,256]{2,1,0:T(8,128)S(1)}, u32[]{:S(2)}) copy-start(f32[9,192,256]{2,1,0:T(8,128)S(1)} %copy.50) | copy-start | bytes 5308420
  43.0 40.9 %collective-permute-start = (f32[9,192,256]{2,1,0:T(8,128)S(1)}, f32[9,192,256]{2,1,0:T(8,128)}, u32[]{:S(2)}, u32[]{:S(2)}) collective-permute-start(f32[9,192,256]{2,1,0:T(8,128)S(1)} %copy.50), channel_id=1, source_target_pairs={{0,8},{8,16},{16,24},{24,32},{32,40},{40,48},{48,56},{56,64},{64,7... | collective-permute-start | bytes 5308424 | tf_op jit(solution)/shard_map/ppermute | solution.py:24
  44.6 42.8 %collective-permute-start.1 = (f32[9,192,256]{2,1,0:T(8,128)S(1)}, f32[9,192,256]{2,1,0:T(8,128)}, u32[]{:S(2)}, u32[]{:S(2)}) collective-permute-start(f32[9,192,256]{2,1,0:T(8,128)S(1)} %copy.50), channel_id=1, source_target_pairs={{8,0},{16,8},{24,16},{32,24},{40,32},{48,40},{56,48},{64,56},{72,6... | collective-permute-start | bytes 5308424 | tf_op jit(solution)/shard_map/ppermute | solution.py:25
  68.9 15.1 %copy-start.1 = (f32[9,27,24,192]{3,2,1,0:T(8,128)S(1)}, f32[9,27,24,192]{3,2,1,0:T(8,128)}, u32[]{:S(2)}) copy-start(f32[9,27,24,192]{3,2,1,0:T(8,128)} %gather.7) | copy-start | bytes 13436932
  120.9 30.3 %copy-start.8 = (f32[1728,32]{0,1:T(8,128)S(1)}, f32[1728,32]{0,1:T(8,128)}, u32[]{:S(2)}) copy-start(f32[1728,32]{0,1:T(8,128)} %reshape.104) | copy-start | bytes 663556
  122.8 6.2 %collective-permute-start.2 = (f32[256,32]{0,1:T(8,128)S(1)}, f32[256,32]{0,1:T(8,128)S(1)}, u32[]{:S(2)}, u32[]{:S(2)}) collective-permute-start(f32[256,32]{0,1:T(8,128)S(1)} %convolution_bitcast_fusion.3), channel_id=1, source_target_pairs={{0,8},{8,0},{16,24},{24,16},{32,40},{40,32},{48,56},{56,48},{64,72... | collective-permute-start | bytes 98312 | tf_op jit(solution)/shard_map/ppermute | solution.py:15
  129.1 5.4 %collective-permute-start.3 = (f32[256,32]{0,1:T(8,128)S(1)}, f32[256,32]{0,1:T(8,128)S(1)}, u32[]{:S(2)}, u32[]{:S(2)}) collective-permute-start(f32[256,32]{0,1:T(8,128)S(1)} %add.128), channel_id=1, source_target_pairs={{0,16},{8,24},{16,0},{24,8},{32,48},{40,56},{48,32},{56,40},{64,80... | collective-permute-start | bytes 98312 | tf_op jit(solution)/shard_map/ppermute | solution.py:15
  134.5 4.1 %collective-permute-start.4 = (f32[256,32]{0,1:T(8,128)S(1)}, f32[256,32]{0,1:T(8,128)S(1)}, u32[]{:S(2)}, u32[]{:S(2)}) collective-permute-start(f32[256,32]{0,1:T(8,128)S(1)} %add.129), channel_id=1, source_target_pairs={{0,32},{8,40},{16,48},{24,56},{32,0},{40,8},{48,16},{56,24},{64,96... | collective-permute-start | bytes 98312 | tf_op jit(solution)/shard_map/ppermute | solution.py:15
  138.6 4.8 %collective-permute-start.5 = (f32[256,32]{0,1:T(8,128)S(1)}, f32[256,32]{0,1:T(8,128)S(1)}, u32[]{:S(2)}, u32[]{:S(2)}) collective-permute-start(f32[256,32]{0,1:T(8,128)S(1)} %add.130), channel_id=1, source_target_pairs={{0,64},{8,72},{16,80},{24,88},{32,96},{40,104},{48,112},{56,120},{... | collective-permute-start | bytes 98312 | tf_op jit(solution)/shard_map/ppermute | solution.py:15
  143.4 7.8 %collective-permute-start.6 = (f32[256,32]{0,1:T(8,128)S(1)}, f32[256,32]{0,1:T(8,128)S(1)}, u32[]{:S(2)}, u32[]{:S(2)}) collective-permute-start(f32[256,32]{0,1:T(8,128)S(1)} %add.131), channel_id=1, source_target_pairs={{0,128},{8,136},{16,144},{24,152},{32,160},{40,168},{48,176},{56,1... | collective-permute-start | bytes 98312 | tf_op jit(solution)/shard_map/ppermute | solution.py:15
  157.1 32.1 %copy-start.4 = (f32[9,24,8,32]{1,2,0,3:T(8,128)S(1)}, f32[9,24,8,32]{1,2,0,3:T(8,128)}, u32[]{:S(2)}) copy-start(f32[9,24,8,32]{1,2,0,3:T(8,128)} %copy.77) | copy-start | bytes 663556
  157.1 33.1 %copy-start.7 = (f32[9,192,32]{1,2,0:T(8,128)S(1)}, f32[9,192,32]{1,2,0:T(8,128)}, u32[]{:S(2)}) copy-start(f32[9,192,32]{1,2,0:T(8,128)} %convolution_bitcast_fusion.2) | copy-start | bytes 663556
  187.0 41.1 %collective-permute-start.7 = (f32[9,192,256]{2,1,0:T(8,128)}, f32[9,192,256]{2,1,0:T(8,128)}, u32[]{:S(2)}, u32[]{:S(2)}) collective-permute-start(f32[9,192,256]{2,1,0:T(8,128)} %copy.57), channel_id=1, source_target_pairs={{0,8},{8,16},{16,24},{24,32},{32,40},{40,48},{48,56},{56,64},{64,7... | collective-permute-start | bytes 5308424 | tf_op jit(solution)/shard_map/ppermute | solution.py:24
  188.4 43.6 %collective-permute-start.8 = (f32[9,192,256]{2,1,0:T(8,128)}, f32[9,192,256]{2,1,0:T(8,128)}, u32[]{:S(2)}, u32[]{:S(2)}) collective-permute-start(f32[9,192,256]{2,1,0:T(8,128)} %copy.57), channel_id=1, source_target_pairs={{8,0},{16,8},{24,16},{32,24},{40,32},{48,40},{56,48},{64,56},{72,6... | collective-permute-start | bytes 5308424 | tf_op jit(solution)/shard_map/ppermute | solution.py:25
  191.2 40.9 %slice-start = ((s8[5971968]{0:T(1024)(128)(4,1)}), s8[1777664]{0:T(1024)(128)(4,1)S(1)}, s32[]{:S(2)}) async-start(s8[5971968]{0:T(1024)(128)(4,1)} %bitcast.125), calls=%async_computation.4 | async-start | bytes 3555328
  193.2 38.9 %slice-start.1 = ((s8[5971968]{0:T(1024)(128)(4,1)}), s8[4194304]{0:T(1024)(128)(4,1)S(1)}, s32[]{:S(2)}) async-start(s8[5971968]{0:T(1024)(128)(4,1)} %bitcast.125), calls=%async_computation.5 | async-start | bytes 8388608
  242.7 10.9 %all-to-all-start.1 = ((f32[8,1,6912]{2,1,0:T(1,128)}), f32[8,1,6912]{2,1,0:T(1,128)S(1)}, u32[]{:S(2)}, u32[]{:S(2)}) async-start(f32[8,1,6912]{2,1,0:T(1,128)} %reshape.135), calls=%async_computation.1 | async-start | bytes 442368 | tf_op jit(solution)/shard_map/all_to_all | solution.py:57
  259.9 3.8 %copy-start.3 = (f32[9,192,256]{2,1,0:T(8,128)S(1)}, f32[9,192,256]{2,1,0:T(8,128)}, u32[]{:S(2)}) copy-start(f32[9,192,256]{2,1,0:T(8,128)} %copy-done.2) | copy-start | bytes 5308420
  271.1 44.2 %copy-start.6 = (f32[9,192,32]{1,0,2:T(8,128)S(1)}, f32[9,192,32]{1,0,2:T(8,128)}, u32[]{:S(2)}) copy-start(f32[9,192,32]{1,0,2:T(8,128)} %copy.56) | copy-start | bytes 663556
  271.1 45.1 %copy-start.5 = (f32[9,24,8,32]{1,2,0,3:T(8,128)S(1)}, f32[9,24,8,32]{1,2,0,3:T(8,128)}, u32[]{:S(2)}) copy-start(f32[9,24,8,32]{1,2,0,3:T(8,128)} %copy.76) | copy-start | bytes 663556
  271.1 10.4 %collective-permute-start.9 = (f32[65792]{0:T(1024)S(1)}, f32[65792]{0:T(1024)S(1)}, u32[]{:S(2)}, u32[]{:S(2)}) collective-permute-start(f32[65792]{0:T(1024)S(1)} %pad_maximum_fusion.1), channel_id=1, source_target_pairs={{0,8},{8,0},{16,24},{24,16},{32,40},{40,32},{48,56},{56,48},{64,72... | collective-permute-start | bytes 789512 | tf_op jit(solution)/shard_map/ppermute | solution.py:15
  281.6 8.8 %collective-permute-start.10 = (f32[65792]{0:T(1024)S(1)}, f32[65792]{0:T(1024)S(1)}, u32[]{:S(2)}, u32[]{:S(2)}) collective-permute-start(f32[65792]{0:T(1024)S(1)} %fusion.73), channel_id=1, source_target_pairs={{0,16},{8,24},{16,0},{24,8},{32,48},{40,56},{48,32},{56,40},{64,80... | collective-permute-start | bytes 789512 | tf_op jit(solution)/shard_map/ppermute | solution.py:15
  290.5 6.5 %collective-permute-start.11 = (f32[65792]{0:T(1024)S(1)}, f32[65792]{0:T(1024)S(1)}, u32[]{:S(2)}, u32[]{:S(2)}) collective-permute-start(f32[65792]{0:T(1024)S(1)} %add.136), channel_id=1, source_target_pairs={{0,32},{8,40},{16,48},{24,56},{32,0},{40,8},{48,16},{56,24},{64,96... | collective-permute-start | bytes 789512 | tf_op jit(solution)/shard_map/ppermute | solution.py:15
  297.0 11.9 %collective-permute-start.12 = (f32[65792]{0:T(1024)S(1)}, f32[65792]{0:T(1024)S(1)}, u32[]{:S(2)}, u32[]{:S(2)}) collective-permute-start(f32[65792]{0:T(1024)S(1)} %add.137), channel_id=1, source_target_pairs={{0,64},{8,72},{16,80},{24,88},{32,96},{40,104},{48,112},{56,120},{... | collective-permute-start | bytes 789512 | tf_op jit(solution)/shard_map/ppermute | solution.py:15
  309.7 17.7 %collective-permute-start.13 = (f32[65792]{0:T(1024)}, f32[65792]{0:T(1024)}, u32[]{:S(2)}, u32[]{:S(2)}) collective-permute-start(f32[65792]{0:T(1024)} %add.138), channel_id=1, source_target_pairs={{0,128},{8,136},{16,144},{24,152},{32,160},{40,168},{48,176},{56,1... | collective-permute-start | bytes 789512 | tf_op jit(solution)/shard_map/ppermute | solution.py:15
  329.1 3.7 %copy-start.9 = (f32[1728,32]{0,1:T(8,128)S(1)}, f32[1728,32]{0,1:T(8,128)}, u32[]{:S(2)}) copy-start(f32[1728,32]{0,1:T(8,128)} %reshape.107) | copy-start | bytes 663556
Sparse Core Ops, SparseCore 0:
  9.8 31.0 all-gather.2
  157.2 26.6 all-gather.4
where the time goes:
time: 348 us; the launch traced here: 341 us
  waiting for transfers between devices  165 us (47%)
  local copies, waits for them, and re-layouts  68.5 us (20%)
  matrix products  39.1 us (11%)
  starting transfers between devices  30.3 us (9%)
  between operations  14.7 us (4%)
  other arithmetic  12.6 us (4%)
  blocking collectives  11.1 us (3%)
    ppermute x10, waiting for transfers between devices, space_sum(): value = value + lax.ppermute(value, 'space', pairs)  60.5 us
    ppermute x2, waiting for transfers between devices, halo(): low = lax.ppermute(block[block.shape[0] - width:], 'space', forward)  40.6 us
    all_gather x1, waiting for transfers between devices, local(): full_x = lax.all_gather(stacked_x, 'mode', axis=2, tiled=True)  31.6 us
    all_gather x1, waiting for transfers between devices, local(): full_s = lax.all_gather(search_raw, 'mode', axis=2, tiled=True)  26.9 us
    dot_general x6, matrix products, apply_dense(): jnp.einsum('ijrc,jcm->irm', coeffs, field, precision=HIGHEST, preferred_e...  25 us
    ppermute x10, starting transfers between devices, space_sum(): value = value + lax.ppermute(value, 'space', pairs)  22.1 us
    gather x2, local copies, waits for them, and re-layouts, dense_rows(): jnp.take(table, flat, axis=0).reshape(block_rows, ext_blocks, rows, cols)  15.3 us
    unnamed x32, local copies, waits for them, and re-layouts  12.6 us
  transfers between devices with their start and end apart: 17, of which 15 were waited for; matrix products, arithmetic and copies ran while one was open for 14% of the time, Pallas kernels for 0%

commit v1 on v0

--- a/solution.py
+++ b/solution.py
@@ -97,7 +97,8 @@
         precision=HIGHEST,
         preferred_element_type=jnp.float32,
     )
-    full_s = lax.all_gather(search_raw, "mode", axis=2, tiled=True)
+    stack = jnp.stack([search_raw] * lax.axis_size("mode"))
+    full_s = jnp.concatenate(lax.all_to_all(stack, "mode", 0, 0), axis=2)
     low_s, high_s = halo(full_s, CELLS)
     image_s = apply_dense(dense, low_s, full_s, high_s)
     flat_s = full_s.reshape(row_count, mode_count)

time: 348 us -> 360 us (1.034)
  blocking collectives: 11.1 us -> 43.5 us
  waiting for transfers between devices: 165 us -> 134 us
  local copies, waits for them, and re-layouts: 68.5 us -> 77.6 us
  starting transfers between devices: 30.3 us -> 36.3 us
    all_to_all x0 -> x1, blocking collectives: none -> 32.5 us  [local(): full_s = jnp.concatenate(lax.all_to_all(stack, 'mode', 0, 0), axis=2)]
    all_gather x1 -> x0, waiting for transfers between devices: 26.9 us -> none  [local(): full_s = lax.all_gather(search_raw, 'mode', axis=2, tiled=True)]
    reshape x0 -> x3, local copies, waits for them, and re-layouts: none -> 10.1 us  [local(): full_s = jnp.concatenate(lax.all_to_all(stack, 'mode', 0, 0), axis=2)]
    another operation x1 -> x4, local copies, waits for them, and re-layouts: 0.01 us -> 7.58 us  [the longest x2 7.3 us: local(): flat_s = full_s.reshape(row_count, mode_count)]
    ppermute x10, starting transfers between devices: 22.1 us -> 28.2 us  [space_sum(): value = value + lax.ppermute(value, 'space', pairs)]
    all_to_all x1, waiting for transfers between devices: 5.08 us -> 0.01 us  [apply_dense(): lax.all_to_all(total, 'mode', split_axis=2, concat_axis=1, tiled=True)]
    ppermute x2, waiting for transfers between devices: 0.01 us -> 4.47 us  [halo(): high = lax.ppermute(block[:width], 'space', backward)]
    ppermute x2, waiting for transfers between devices: 40.6 us -> 36.7 us  [halo(): low = lax.ppermute(block[block.shape[0] - width:], 'space', forward)]
  transfers between devices with their start and end apart: 17 -> 16, of which waited for: 15 -> 14; matrix products, arithmetic and copies ran while one was open for 14% -> 16% of each run, Pallas kernels for 0% -> 0%
where the time goes in v1:
time: 360 us; the launch traced here: 353 us
  waiting for transfers between devices  134 us (37%)
  local copies, waits for them, and re-layouts  77.6 us (22%)
  blocking collectives  43.5 us (12%)
  matrix products  36.9 us (10%)
  starting transfers between devices  36.3 us (10%)
  between operations  14.6 us (4%)
  other arithmetic  10.6 us (3%)
    ppermute x10, waiting for transfers between devices, space_sum(): value = value + lax.ppermute(value, 'space', pairs)  61 us
    ppermute x2, waiting for transfers between devices, halo(): low = lax.ppermute(block[block.shape[0] - width:], 'space', forward)  36.7 us
    all_to_all x1, blocking collectives, local(): full_s = jnp.concatenate(lax.all_to_all(stack, 'mode', 0, 0), axis=2)  32.5 us
    all_gather x1, waiting for transfers between devices, local(): full_x = lax.all_gather(stacked_x, 'mode', axis=2, tiled=True)  31.6 us
    ppermute x10, starting transfers between devices, space_sum(): value = value + lax.ppermute(value, 'space', pairs)  28.2 us
    dot_general x6, matrix products, apply_dense(): jnp.einsum('ijrc,jcm->irm', coeffs, field, precision=HIGHEST, preferred_e...  23.6 us
    gather x2, local copies, waits for them, and re-layouts, dense_rows(): jnp.take(table, flat, axis=0).reshape(block_rows, ext_blocks, rows, cols)  14.9 us
    unnamed x36, local copies, waits for them, and re-layouts  13.2 us
  transfers between devices with their start and end apart: 16, of which 14 were waited for; matrix products, arithmetic and copies ran while one was open for 16% of the time, Pallas kernels for 0%

profile of v1, /device:TPU:2, one launch (start us, length us, event | category | flops | bytes accessed | tf_op | source)
XLA Modules:
  0.0 353.4 jit_solution(12955382183626039952)
XLA Ops:
  7.2 1.2 reshape.109
  9.3 31.6 %all-gather.2.cloned.1.call-done = f32[9,192,256]{1,2,0:T(8,128)} async-done(((f32[9,192,32]{1,2,0:T(8,128)}), f32[9,192,256]{1,2,0:T(8,128)}) %all-gather.2.cloned.1.call-update) | async-done | bytes 1769488 | tf_op jit(solution)/shard_map/all_gather | solution.py:77
  41.0 2.0 copy.54
  43.0 1.5 collective-permute-start
  44.6 6.7 %reshape.108 = f32[243,4608]{1,0:T(8,128)} reshape(f32[9,27,24,192]{3,2,1,0:T(8,128)} %param.5) | data formatting | bytes 8957952 | tf_op jit(solution)/shard_map/reshape | solution.py:38
  53.5 8.4 %gather_fusion = f32[243,4608]{1,0:T(8,128)} fusion(f32[243,4608]{1,0:T(8,128)} %reshape.108, s32[1024]{0:T(1024)S(1)} %pad_clamp_fusion), kind=kCustom, calls=%fused_computation | custom fusion | bytes 8958924 | tf_op jit(solution)/shard_map/jit(_take)/gather | solution.py:39
  61.9 6.5 %gather.7 = f32[9,27,24,192]{3,2,1,0:T(8,128)} reshape(f32[243,4608]{1,0:T(8,128)} %gather_fusion) | data formatting | bytes 8957952 | tf_op jit(solution)/shard_map/jit(_take)/gather | solution.py:39
  68.5 4.6 %fusion.16 = f32[9,24,256]{2,1,0:T(8,128)S(1)} fusion(f32[9,192,256]{1,2,0:T(8,128)} %all-gather.2.cloned.1.call-done, f32[9,27,24,192]{3,2,1,0:T(8,128)} %gather.7, pred[9,27]{1,0:T(8,128)(4,1)S(1)} %get-tuple-element.16, pred[9,27]{1,0:T(8,128)(4,1)S(1)} %fusion.44), kind=kOutput, calls=%fused_computation.24 | convolution fusion | flops 1148857344 | bytes 6470118 | tf_op jit(solution)/shard_map/ijrc,jcm->irm/dot_general | solution.py:53
  73.2 10.8 %collective-permute-done = f32[9,192,256]{2,1,0:T(8,128)} collective-permute-done((f32[9,192,256]{2,1,0:T(8,128)S(1)}, f32[9,192,256]{2,1,0:T(8,128)}, u32[]{:S(2)}, u32[]{:S(2)}) %collective-permute-start) | collective-permute-done | bytes 1769504 | tf_op jit(solution)/shard_map/ppermute | solution.py:24
  83.9 3.5 fusion.34
  87.4 4.5 %collective-permute-done.1 = f32[9,192,256]{2,1,0:T(8,128)} collective-permute-done((f32[9,192,256]{2,1,0:T(8,128)S(1)}, f32[9,192,256]{2,1,0:T(8,128)}, u32[]{:S(2)}, u32[]{:S(2)}) %collective-permute-start.1) | collective-permute-done | bytes 1769504 | tf_op jit(solution)/shard_map/ppermute | solution.py:25
  91.9 4.2 %fusion.31 = f32[9,24,256]{2,1,0:T(8,128)} fusion(f32[9,24,256]{2,1,0:T(8,128)S(1)} %fusion.34, f32[9,192,256]{2,1,0:T(8,128)} %collective-permute-done.1, f32[9,27,24,192]{3,2,1,0:T(8,128)S(1)} %copy-done.2, pred[9,27]{1,0:T(8,128)(4,1)S(1)} %get-tuple-element.16, pred[9,27]{1,0:T(8,128)(4,1)S(1)} %fusion.44), kind=kOutput, calls=%fused_computation.29 | convolution fusion | flops 1148912640 | bytes 6691302 | tf_op jit(solution)/shard_map/ijrc,jcm->irm/dot_general | solution.py:53
  96.0 3.4 copy.56
  99.4 3.1 reshape.140
  102.5 11.1 %all_to_all.35 = f32[8,1,6912]{2,1,0:T(1,128)} all-to-all(f32[8,1,6912]{2,1,0:T(1,128)} %reshape.140), channel_id=1, replica_groups=mesh['space'=32,'mode'=8] {'mode'}, dimensions={0} | all-to-all | bytes 442368 | tf_op jit(solution)/shard_map/all_to_all | solution.py:57
  114.1 2.8 reduce.1
  116.9 2.8 reshape.141
  119.7 3.4 copy.86
  123.1 2.3 reshape.110
  125.4 1.9 convolution_bitcast_fusion.3
  127.4 3.1 collective-permute-start.2
  130.5 1.9 collective-permute-done.2
  132.4 3.5 collective-permute-start.3
  135.8 1.9 collective-permute-done.3
  137.8 1.7 collective-permute-start.4
  139.5 2.2 collective-permute-done.4
  141.7 4.7 %collective-permute-start.5 = (f32[256,32]{0,1:T(8,128)S(1)}, f32[256,32]{0,1:T(8,128)S(1)}, u32[]{:S(2)}, u32[]{:S(2)}) collective-permute-start(f32[256,32]{0,1:T(8,128)S(1)} %add.130), channel_id=1, source_target_pairs={{0,64},{8,72},{16,80},{24,88},{32,96},{40,104},{48,112},{56,120},{... | collective-permute-start | bytes 98312 | tf_op jit(solution)/shard_map/ppermute | solution.py:15
  146.4 1.9 collective-permute-done.5
  148.3 3.8 %collective-permute-start.6 = (f32[256,32]{0,1:T(8,128)S(1)}, f32[256,32]{0,1:T(8,128)S(1)}, u32[]{:S(2)}, u32[]{:S(2)}) collective-permute-start(f32[256,32]{0,1:T(8,128)S(1)} %add.131), channel_id=1, source_target_pairs={{0,128},{8,136},{16,144},{24,152},{32,160},{40,168},{48,176},{56,1... | collective-permute-start | bytes 98312 | tf_op jit(solution)/shard_map/ppermute | solution.py:15
  152.1 4.0 %collective-permute-done.6 = f32[256,32]{0,1:T(8,128)S(1)} collective-permute-done((f32[256,32]{0,1:T(8,128)S(1)}, f32[256,32]{0,1:T(8,128)S(1)}, u32[]{:S(2)}, u32[]{:S(2)}) %collective-permute-start.6) | collective-permute-done | bytes 32800 | tf_op jit(solution)/shard_map/ppermute | solution.py:15
  156.1 2.3 fusion.10
  158.4 1.1 reshape.112
  159.5 1.7 convolution_bitcast_fusion.2
  161.5 32.5 %all_to_all.36 = f32[8,9,192,32]{2,3,1,0:T(8,128)S(1)} all-to-all(f32[8,9,192,32]{2,3,1,0:T(8,128)S(1)} %stack.8), channel_id=1, replica_groups=mesh['space'=32,'mode'=8] {'mode'}, dimensions={0} | all-to-all | bytes 3538944 | tf_op jit(solution)/shard_map/all_to_all | solution.py:101
  194.0 1.7 copy.64
  196.2 3.1 copy.66
  199.3 1.9 collective-permute-start.7
  201.7 1.0 stack_reshape.10
  203.8 5.4 %copy.61 = f32[9,192,8,32]{1,0,3,2:T(8,128)} copy(f32[9,192,8,32]{1,3,0,2:T(8,128)} %bitcast.130) | data formatting | bytes 3538944 | tf_op jit(solution)/shard_map/reshape | solution.py:101
  209.2 4.5 %fusion.15 = f32[9,24,256]{2,1,0:T(8,128)S(1)} fusion(f32[9,192,256,1]{1,2,0,3:T(8,128)} %bitcast.135, f32[9,27,24,192]{3,2,1,0:T(8,128)} %gather.7, pred[9,27]{1,0:T(8,128)(4,1)S(1)} %get-tuple-element.16, pred[9,27]{1,0:T(8,128)(4,1)S(1)} %fusion.44), kind=kOutput, calls=%fused_computation.23 | convolution fusion | flops 1148857344 | bytes 6470118 | tf_op jit(solution)/shard_map/ijrc,jcm->irm/dot_general | solution.py:53
  213.6 25.9 %collective-permute-done.7 = f32[9,192,256]{2,1,0:T(8,128)} collective-permute-done((f32[9,192,256]{2,1,0:T(8,128)}, f32[9,192,256]{2,1,0:T(8,128)}, u32[]{:S(2)}, u32[]{:S(2)}) %collective-permute-start.7) | collective-permute-done | bytes 1769504 | tf_op jit(solution)/shard_map/ppermute | solution.py:24
  239.6 3.4 fusion.40
  243.0 3.4 fusion.37
  246.5 2.5 copy.68
  248.9 3.1 reshape.142
  252.0 3.6 %all-to-all-start.2 = ((f32[8,1,6912]{2,1,0:T(1,128)}), f32[8,1,6912]{2,1,0:T(1,128)S(1)}, u32[]{:S(2)}, u32[]{:S(2)}) async-start(f32[8,1,6912]{2,1,0:T(1,128)} %reshape.142), calls=%async_computation.2 | async-start | bytes 442368 | tf_op jit(solution)/shard_map/all_to_all | solution.py:57
  255.6 1.9 multiply_reduce_fusion
  257.6 4.6 %reshape_reshape.3 = f32[1728,256]{0,1:T(8,128)} reshape(f32[9,192,8,32]{1,0,3,2:T(8,128)} %copy.61) | data formatting | bytes 3538944 | tf_op jit(solution)/shard_map/reshape;reshape | solution.py:104
  262.2 2.7 copy.62
  264.9 1.2 reduce.2
  266.1 1.9 reshape.143
  268.0 2.3 copy.85
  270.3 1.0 stack_reshape.11
  271.4 1.1 pad_maximum_fusion
  272.5 7.3 %convolution_bitcast_fusion = f32[65536]{0:T(1024)S(1)} fusion(f32[1728,128]{0,1:T(8,128)S(1)} %bitcast.144, f32[1728,256]{1,0:T(8,128)} %copy.62, f32[1728,256]{1,0:T(8,128)S(1)} %bitcast.133), kind=kOutput, calls=%fused_computation.1 | convolution fusion | flops 1359839232 | bytes 4685824
  279.9 5.5 %collective-permute-start.9 = (f32[65792]{0:T(1024)S(1)}, f32[65792]{0:T(1024)S(1)}, u32[]{:S(2)}, u32[]{:S(2)}) collective-permute-start(f32[65792]{0:T(1024)S(1)} %pad_maximum_fusion.1), channel_id=1, source_target_pairs={{0,8},{8,0},{16,24},{24,16},{32,40},{40,32},{48,56},{56,48},{64,72... | collective-permute-start | bytes 789512 | tf_op jit(solution)/shard_map/ppermute | solution.py:15
  285.4 7.0 %collective-permute-done.9 = f32[65792]{0:T(1024)S(1)} collective-permute-done((f32[65792]{0:T(1024)S(1)}, f32[65792]{0:T(1024)S(1)}, u32[]{:S(2)}, u32[]{:S(2)}) %collective-permute-start.9) | collective-permute-done | bytes 263200 | tf_op jit(solution)/shard_map/ppermute | solution.py:15
  292.5 9.7 %collective-permute-done.10 = f32[65792]{0:T(1024)S(1)} collective-permute-done((f32[65792]{0:T(1024)S(1)}, f32[65792]{0:T(1024)S(1)}, u32[]{:S(2)}, u32[]{:S(2)}) %collective-permute-start.10) | collective-permute-done | bytes 263200 | tf_op jit(solution)/shard_map/ppermute | solution.py:15
  302.3 7.3 %collective-permute-done.11 = f32[65792]{0:T(1024)S(1)} collective-permute-done((f32[65792]{0:T(1024)S(1)}, f32[65792]{0:T(1024)S(1)}, u32[]{:S(2)}, u32[]{:S(2)}) %collective-permute-start.11) | collective-permute-done | bytes 263200 | tf_op jit(solution)/shard_map/ppermute | solution.py:15
  309.6 1.0 collective-permute-start.12
  310.7 12.1 %collective-permute-done.12 = f32[65792]{0:T(1024)S(1)} collective-permute-done((f32[65792]{0:T(1024)S(1)}, f32[65792]{0:T(1024)S(1)}, u32[]{:S(2)}, u32[]{:S(2)}) %collective-permute-start.12) | collective-permute-done | bytes 263200 | tf_op jit(solution)/shard_map/ppermute | solution.py:15
  322.8 4.7 %collective-permute-start.13 = (f32[65792]{0:T(1024)S(1)}, f32[65792]{0:T(1024)S(1)}, u32[]{:S(2)}, u32[]{:S(2)}) collective-permute-start(f32[65792]{0:T(1024)S(1)} %add.138), channel_id=1, source_target_pairs={{0,128},{8,136},{16,144},{24,152},{32,160},{40,168},{48,176},{56,1... | collective-permute-start | bytes 789512 | tf_op jit(solution)/shard_map/ppermute | solution.py:15
  328.0 13.1 %collective-permute-done.13 = f32[65792]{0:T(1024)S(1)} collective-permute-done((f32[65792]{0:T(1024)S(1)}, f32[65792]{0:T(1024)S(1)}, u32[]{:S(2)}, u32[]{:S(2)}) %collective-permute-start.13) | collective-permute-done | bytes 263200 | tf_op jit(solution)/shard_map/ppermute | solution.py:15
  341.8 1.5 multiply_multiply_fusion
  (77 shorter events, 10.7 us)
Async XLA Ops:
  7.2 152.3 %copy-start = (f32[9,192,192]{2,1,0:T(8,128)S(1)}, f32[9,192,192]{2,1,0:T(8,128)}, u32[]{:S(2)}) copy-start(f32[9,192,192]{2,1,0:T(8,128)} %param.6) | copy-start | bytes 3981316
  7.2 33.8 %all-gather.2.cloned.1.call-start = ((), (), s32[]{:S(2)}) async-start(), calls=%async_computation.3 | async-start | bytes 2654208 | tf_op jit(solution)/shard_map/all_gather | solution.py:77
  43.0 113.1 %copy-start.4 = (f32[9,192,256]{2,1,0:T(8,128)}, f32[9,192,256]{2,1,0:T(8,128)S(1)}, u32[]{:S(2)}) copy-start(f32[9,192,256]{2,1,0:T(8,128)S(1)} %copy.54) | copy-start | bytes 5308420
  43.0 40.9 %collective-permute-start = (f32[9,192,256]{2,1,0:T(8,128)S(1)}, f32[9,192,256]{2,1,0:T(8,128)}, u32[]{:S(2)}, u32[]{:S(2)}) collective-permute-start(f32[9,192,256]{2,1,0:T(8,128)S(1)} %copy.54), channel_id=1, source_target_pairs={{0,8},{8,16},{16,24},{24,32},{32,40},{40,48},{48,56},{56,64},{64,7... | collective-permute-start | bytes 5308424 | tf_op jit(solution)/shard_map/ppermute | solution.py:24
  44.6 7.3 %copy-start.12 = (s32[9,27]{1,0:T(8,128)S(1)}, s32[9,27]{1,0:T(8,128)}, u32[]{:S(2)}) copy-start(s32[9,27]{1,0:T(8,128)} %param.7) | copy-start | bytes 2920
  51.3 40.6 %collective-permute-start.1 = (f32[9,192,256]{2,1,0:T(8,128)S(1)}, f32[9,192,256]{2,1,0:T(8,128)}, u32[]{:S(2)}, u32[]{:S(2)}) collective-permute-start(f32[9,192,256]{2,1,0:T(8,128)S(1)} %copy.54), channel_id=1, source_target_pairs={{8,0},{16,8},{24,16},{32,24},{40,32},{48,40},{56,48},{64,56},{72,6... | collective-permute-start | bytes 5308424 | tf_op jit(solution)/shard_map/ppermute | solution.py:25
  68.5 15.4 %copy-start.2 = (f32[9,27,24,192]{3,2,1,0:T(8,128)S(1)}, f32[9,27,24,192]{3,2,1,0:T(8,128)}, u32[]{:S(2)}) copy-start(f32[9,27,24,192]{3,2,1,0:T(8,128)} %gather.7) | copy-start | bytes 13436932
  125.4 30.7 %copy-start.9 = (f32[1728,32]{0,1:T(8,128)S(1)}, f32[1728,32]{0,1:T(8,128)}, u32[]{:S(2)}) copy-start(f32[1728,32]{0,1:T(8,128)} %reshape.110) | copy-start | bytes 663556
  127.4 5.0 %collective-permute-start.2 = (f32[256,32]{0,1:T(8,128)S(1)}, f32[256,32]{0,1:T(8,128)S(1)}, u32[]{:S(2)}, u32[]{:S(2)}) collective-permute-start(f32[256,32]{0,1:T(8,128)S(1)} %convolution_bitcast_fusion.3), channel_id=1, source_target_pairs={{0,8},{8,0},{16,24},{24,16},{32,40},{40,32},{48,56},{56,48},{64,72... | collective-permute-start | bytes 98312 | tf_op jit(solution)/shard_map/ppermute | solution.py:15
  132.4 5.4 %collective-permute-start.3 = (f32[256,32]{0,1:T(8,128)S(1)}, f32[256,32]{0,1:T(8,128)S(1)}, u32[]{:S(2)}, u32[]{:S(2)}) collective-permute-start(f32[256,32]{0,1:T(8,128)S(1)} %add.128), channel_id=1, source_target_pairs={{0,16},{8,24},{16,0},{24,8},{32,48},{40,56},{48,32},{56,40},{64,80... | collective-permute-start | bytes 98312 | tf_op jit(solution)/shard_map/ppermute | solution.py:15
  137.8 3.9 %collective-permute-start.4 = (f32[256,32]{0,1:T(8,128)S(1)}, f32[256,32]{0,1:T(8,128)S(1)}, u32[]{:S(2)}, u32[]{:S(2)}) collective-permute-start(f32[256,32]{0,1:T(8,128)S(1)} %add.129), channel_id=1, source_target_pairs={{0,32},{8,40},{16,48},{24,56},{32,0},{40,8},{48,16},{56,24},{64,96... | collective-permute-start | bytes 98312 | tf_op jit(solution)/shard_map/ppermute | solution.py:15
  141.7 6.6 %collective-permute-start.5 = (f32[256,32]{0,1:T(8,128)S(1)}, f32[256,32]{0,1:T(8,128)S(1)}, u32[]{:S(2)}, u32[]{:S(2)}) collective-permute-start(f32[256,32]{0,1:T(8,128)S(1)} %add.130), channel_id=1, source_target_pairs={{0,64},{8,72},{16,80},{24,88},{32,96},{40,104},{48,112},{56,120},{... | collective-permute-start | bytes 98312 | tf_op jit(solution)/shard_map/ppermute | solution.py:15
  148.3 7.8 %collective-permute-start.6 = (f32[256,32]{0,1:T(8,128)S(1)}, f32[256,32]{0,1:T(8,128)S(1)}, u32[]{:S(2)}, u32[]{:S(2)}) collective-permute-start(f32[256,32]{0,1:T(8,128)S(1)} %add.131), channel_id=1, source_target_pairs={{0,128},{8,136},{16,144},{24,152},{32,160},{40,168},{48,176},{56,1... | collective-permute-start | bytes 98312 | tf_op jit(solution)/shard_map/ppermute | solution.py:15
  194.0 2.2 copy-start.3
  196.2 5.5 %copy-start.6 = (f32[9,24,8,32]{1,2,0,3:T(8,128)S(1)}, f32[9,24,8,32]{1,2,0,3:T(8,128)}, u32[]{:S(2)}) copy-start(f32[9,24,8,32]{1,2,0,3:T(8,128)} %copy.86) | copy-start | bytes 663556
  199.3 40.3 %collective-permute-start.7 = (f32[9,192,256]{2,1,0:T(8,128)}, f32[9,192,256]{2,1,0:T(8,128)}, u32[]{:S(2)}, u32[]{:S(2)}) collective-permute-start(f32[9,192,256]{2,1,0:T(8,128)} %copy.66), channel_id=1, source_target_pairs={{0,8},{8,16},{16,24},{24,32},{32,40},{40,48},{48,56},{56,64},{64,7... | collective-permute-start | bytes 5308424 | tf_op jit(solution)/shard_map/ppermute | solution.py:24
  201.1 41.9 %collective-permute-start.8 = (f32[9,192,256]{2,1,0:T(8,128)}, f32[9,192,256]{2,1,0:T(8,128)}, u32[]{:S(2)}, u32[]{:S(2)}) collective-permute-start(f32[9,192,256]{2,1,0:T(8,128)} %copy.66), channel_id=1, source_target_pairs={{8,0},{16,8},{24,16},{32,24},{40,32},{48,40},{56,48},{64,56},{72,6... | collective-permute-start | bytes 5308424 | tf_op jit(solution)/shard_map/ppermute | solution.py:25
  202.9 6.2 %copy-start.7 = (f32[9,192,32]{1,0,2:T(8,128)}, f32[9,192,32]{1,0,2:T(8,128)S(1)}, u32[]{:S(2)}) copy-start(f32[9,192,32]{1,0,2:T(8,128)S(1)} %copy.60) | copy-start | bytes 663556
  203.0 36.6 %slice-start = ((s8[5971968]{0:T(1024)(128)(4,1)}), s8[1777664]{0:T(1024)(128)(4,1)S(1)}, s32[]{:S(2)}) async-start(s8[5971968]{0:T(1024)(128)(4,1)} %bitcast.127), calls=%async_computation.4 | async-start | bytes 3555328
  203.8 35.8 %slice-start.1 = ((s8[5971968]{0:T(1024)(128)(4,1)}), s8[4194304]{0:T(1024)(128)(4,1)S(1)}, s32[]{:S(2)}) async-start(s8[5971968]{0:T(1024)(128)(4,1)} %bitcast.127), calls=%async_computation.5 | async-start | bytes 8388608
  252.0 12.9 %all-to-all-start.2 = ((f32[8,1,6912]{2,1,0:T(1,128)}), f32[8,1,6912]{2,1,0:T(1,128)S(1)}, u32[]{:S(2)}, u32[]{:S(2)}) async-start(f32[8,1,6912]{2,1,0:T(1,128)} %reshape.142), calls=%async_computation.2 | async-start | bytes 442368 | tf_op jit(solution)/shard_map/all_to_all | solution.py:57
  268.0 3.4 copy-start.10
  268.0 3.4 copy-start.11
  270.3 2.2 copy-start.5
  279.9 47.6 %copy-start.8 = (f32[9,192,32]{1,0,2:T(8,128)S(1)}, f32[9,192,32]{1,0,2:T(8,128)}, u32[]{:S(2)}) copy-start(f32[9,192,32]{1,0,2:T(8,128)} %copy-done.7) | copy-start | bytes 663556
  279.9 12.5 %collective-permute-start.9 = (f32[65792]{0:T(1024)S(1)}, f32[65792]{0:T(1024)S(1)}, u32[]{:S(2)}, u32[]{:S(2)}) collective-permute-start(f32[65792]{0:T(1024)S(1)} %pad_maximum_fusion.1), channel_id=1, source_target_pairs={{0,8},{8,0},{16,24},{24,16},{32,40},{40,32},{48,56},{56,48},{64,72... | collective-permute-start | bytes 789512 | tf_op jit(solution)/shard_map/ppermute | solution.py:15
  292.4 9.8 %collective-permute-start.10 = (f32[65792]{0:T(1024)S(1)}, f32[65792]{0:T(1024)S(1)}, u32[]{:S(2)}, u32[]{:S(2)}) collective-permute-start(f32[65792]{0:T(1024)S(1)} %fusion.70), channel_id=1, source_target_pairs={{0,16},{8,24},{16,0},{24,8},{32,48},{40,56},{48,32},{56,40},{64,80... | collective-permute-start | bytes 789512 | tf_op jit(solution)/shard_map/ppermute | solution.py:15
  302.2 7.4 %collective-permute-start.11 = (f32[65792]{0:T(1024)S(1)}, f32[65792]{0:T(1024)S(1)}, u32[]{:S(2)}, u32[]{:S(2)}) collective-permute-start(f32[65792]{0:T(1024)S(1)} %add.136), channel_id=1, source_target_pairs={{0,32},{8,40},{16,48},{24,56},{32,0},{40,8},{48,16},{56,24},{64,96... | collective-permute-start | bytes 789512 | tf_op jit(solution)/shard_map/ppermute | solution.py:15
  309.6 13.1 %collective-permute-start.12 = (f32[65792]{0:T(1024)S(1)}, f32[65792]{0:T(1024)S(1)}, u32[]{:S(2)}, u32[]{:S(2)}) collective-permute-start(f32[65792]{0:T(1024)S(1)} %add.137), channel_id=1, source_target_pairs={{0,64},{8,72},{16,80},{24,88},{32,96},{40,104},{48,112},{56,120},{... | collective-permute-start | bytes 789512 | tf_op jit(solution)/shard_map/ppermute | solution.py:15
  322.8 18.3 %collective-permute-start.13 = (f32[65792]{0:T(1024)S(1)}, f32[65792]{0:T(1024)S(1)}, u32[]{:S(2)}, u32[]{:S(2)}) collective-permute-start(f32[65792]{0:T(1024)S(1)} %add.138), channel_id=1, source_target_pairs={{0,128},{8,136},{16,144},{24,152},{32,160},{40,168},{48,176},{56,1... | collective-permute-start | bytes 789512 | tf_op jit(solution)/shard_map/ppermute | solution.py:15
  341.8 4.5 %copy-start.1 = (f32[9,192,192]{2,1,0:T(8,128)S(1)}, f32[9,192,192]{2,1,0:T(8,128)}, u32[]{:S(2)}) copy-start(f32[9,192,192]{2,1,0:T(8,128)} %param.6) | copy-start | bytes 3981316
Sparse Core Ops, SparseCore 0:
  9.8 31.0 all-gather.1
